TPU v7x, 256 devices: a whole 4x4x8 slice. The times are simulated.
256 devices in a mesh: gx: 8 (over x, core), yz: 32 (over z, y).
Axes of the slice: x: 4, y: 4, z: 8, core: 2. Of those that a mesh axis runs over, the one named last changes fastest.
Arguments:
- velocity: float32 [3, 256, 512, 128], P(None, 'gx', 'yz'), may hold values from -6 to 6
- old_pressure: float32 [256, 512, 128], P('gx', 'yz'), may hold values from -3 to 3
- delta_weight: bfloat16 [8, 1024, 128, 128], P('gx', 'yz'), may hold values from -0.5 to 0.5
- marker_target: float32 [8, 1024, 3, 128], P('gx', 'yz'), may hold values from -6 to 6
- pair_owner: int32 [8, 1024, 1], P('gx', 'yz'), may hold values from 0 to 31; in each aligned block of 32 rows (0 to 31, 32 to 63, ..., all dimensions but the last counted through in order) at most 4 rows name the same one
- pair_grain: int32 [8, 1024], P('gx', 'yz'), may hold values from 0 to 31
- box_anchor: int32 [8, 1024, 3], P('gx', 'yz'), may hold values from 0 to 120, as said below
Outputs:
- new_velocity: float32 [3, 256, 512, 128], P(None, 'gx', 'yz')
- pressure: float32 [256, 512, 128], P('gx', 'yz')
Inputs may be any that keep to these rules, and one draw needn't show every extreme that they name: Block r of slab i lies on tile r // 32 of that slab; its grain is owned by tile pair_owner of the same slab. Among the 32 blocks of one tile at most 4 name the same owner, and some tile reaches 4. `pair_grain`: blocks of one slab with equal owner and grain slot belong to one grain. `box_anchor`: column 0 is at most 28, column 1 at most 12, column 2 at most 120, and each of these is reached, so every box lies inside its tile.
All inputs are finite; a program needn't handle non-finite values.
Results may differ from a plain program's by a relative error of at most 0.002.
Values may be sent and summed in bfloat16 or wider, within the bound.
No kernel may reach another device: no remote copies, remote signals or barrier semaphores. Data moves between devices by JAX's collectives and lax.ppermute only.
A program may use at most 128 MiB of HBM per device.

v0:
```python
import jax
import jax.numpy as jnp
from jax import lax
from jax.sharding import PartitionSpec as P

BX = 4
BZ = 4
BY = 8
step_size = 0.1
viscosity = 1.5


def extended(block, sides, width):
    for axis, dim in sides:
        count = lax.axis_size(axis)
        forward = [(i, i + 1) for i in range(count - 1)]
        forward.append((count - 1, 0))
        backward = [(target, source) for source, target in forward]
        low = lax.ppermute(
            lax.slice_in_dim(block, block.shape[dim] - width, None, axis=dim), axis, forward
        )
        high = lax.ppermute(lax.slice_in_dim(block, 0, width, axis=dim), axis, backward)
        block = jnp.concatenate([low, block, high], axis=dim)
    return block


def inner(padded):
    return padded[..., 1:-1, 1:-1, :]


def along_x(padded):
    return 0.5 * (padded[..., 2:, 1:-1, :] - padded[..., :-2, 1:-1, :])


def along_z(padded):
    return 0.5 * (padded[..., 1:-1, 2:, :] - padded[..., 1:-1, :-2, :])


def along_y(field):
    return 0.5 * (jnp.roll(field, -1, -1) - jnp.roll(field, 1, -1))


def neighbours(padded):
    middle = inner(padded)
    total = padded[..., 2:, 1:-1, :] + padded[..., :-2, 1:-1, :]
    total = total + padded[..., 1:-1, 2:, :] + padded[..., 1:-1, :-2, :]
    return total + jnp.roll(middle, 1, -1) + jnp.roll(middle, -1, -1)


def gradient_of(padded):
    middle = inner(padded)
    return jnp.stack([along_x(padded), along_y(middle), along_z(padded)])


def predict(flow_padded):
    velocity_padded = flow_padded[:3]
    pressure_padded = flow_padded[3]
    current = inner(velocity_padded)
    laplace = neighbours(velocity_padded) - 6.0 * current
    advect = current[0] * along_x(velocity_padded)
    return current + step_size * (viscosity * laplace - advect) - gradient_of(pressure_padded)


def kernel_box_cells(anchors, box_x, box_z, box_y):
    steps_x = jnp.arange(box_x, dtype=jnp.int32)
    steps_z = jnp.arange(box_z, dtype=jnp.int32)
    steps_y = jnp.arange(box_y, dtype=jnp.int32)
    cell_x = anchors[:, 0, None, None, None] + steps_x[None, :, None, None]
    cell_z = anchors[:, 1, None, None, None] + steps_z[None, None, :, None]
    cell_y = anchors[:, 2, None, None, None] + steps_y[None, None, None, :]
    return (cell_x, cell_z, cell_y)


def walls(padded, vertical_dim):
    tile_index = lax.axis_index("yz")
    tile_total = lax.axis_size("yz")
    extent = padded.shape[vertical_dim]
    position = lax.broadcasted_iota(jnp.int32, padded.shape, vertical_dim)
    bottom_rim = jnp.logical_and(position == 0, tile_index == 0)
    top_rim = jnp.logical_and(position == extent - 1, tile_index == tile_total - 1)
    return jnp.where(jnp.logical_or(bottom_rim, top_rim), jnp.zeros((), padded.dtype), padded)


def pressure_cycle(pressure):
    padded = extended(pressure, (("gx", 0), ("yz", 1)), 1)
    return walls(padded, 1)


def body(velocity, old_pressure, delta_weight, marker_target, pair_owner, pair_grain, box_anchor):
    flow_fields = jnp.concatenate([velocity, old_pressure[None]], 0)
    flow_padded = walls(extended(flow_fields, (("gx", 1), ("yz", 2)), 1), 2)
    predicted = predict(flow_padded)
    anchors = box_anchor[0]
    owners = pair_owner[0, :, 0]
    grains = pair_grain[0]
    delta_weights = delta_weight[0]
    grain_slots = marker_target.shape[1]
    pair_total = anchors.shape[0]
    cell_x, cell_z, cell_y = kernel_box_cells(anchors, BX, BZ, BY)
    kernel_box_values = (
        predicted[:, cell_x, cell_z, cell_y].astype(jnp.bfloat16).reshape(3, pair_total, -1)
    )
    partial_force_value = jnp.einsum(
        "eky,iey->eik", delta_weights, kernel_box_values, preferred_element_type=jnp.float32
    )
    row_width = partial_force_value.shape[1] * partial_force_value.shape[2]
    flat_partial = partial_force_value.reshape(pair_total, row_width)
    targets = marker_target[0].reshape(grain_slots, row_width)
    slot_numbers = jnp.arange(grain_slots, dtype=jnp.int32)
    all_partial, all_owner, all_grain = (
        lax.all_gather(flat_partial, "yz", axis=0, tiled=True),
        lax.all_gather(owners, "yz", axis=0, tiled=True),
        lax.all_gather(grains, "yz", axis=0, tiled=True),
    )
    own_tile = lax.axis_index("yz")
    grain_keys = jnp.where(all_owner == own_tile, all_grain, grain_slots)
    select = (grain_keys[None, :] == slot_numbers[:, None]).astype(jnp.float32)
    summed = jnp.dot(
        select, all_partial, precision=lax.Precision.HIGHEST, preferred_element_type=jnp.float32
    )
    grain_force = (targets - summed).astype(jnp.bfloat16)
    all_force = lax.all_gather(grain_force, "yz", axis=0, tiled=True)
    marker_pair_force = jnp.take(all_force, owners * grain_slots + grains, axis=0)
    spread_force = jnp.einsum(
        "zwx,znw->nzx",
        delta_weights,
        marker_pair_force.reshape(pair_total, 3, -1),
        preferred_element_type=jnp.float32,
    )
    spread_force = spread_force.reshape(3, pair_total, BX, BZ, BY)
    forced_velocity = predicted + jnp.zeros_like(predicted).at[:, cell_x, cell_z, cell_y].add(
        spread_force
    )
    forced_padded = walls(extended(forced_velocity, (("gx", 1), ("yz", 2)), 1), 2)
    divergence = along_x(forced_padded[0]) + along_y(forced_velocity[1]) + along_z(forced_padded[2])
    first_padded = pressure_cycle(old_pressure)
    pressure = (neighbours(first_padded) - divergence) / 6.0
    pressure = (neighbours(pressure_cycle(pressure)) - divergence) / 6.0
    new_velocity = forced_velocity - gradient_of(pressure_cycle(pressure))
    return (new_velocity, pressure)


def solution(mesh):
    placed = (
        P(None, "gx", "yz", None),
        P("gx", "yz", None),
        P("gx", "yz", None, None),
        P("gx", "yz", None, None),
        P("gx", "yz", None),
        P("gx", "yz"),
        P("gx", "yz", None),
    )
    return jax.shard_map(
        body,
        mesh=mesh,
        in_specs=placed,
        out_specs=(P(None, "gx", "yz", None), P("gx", "yz", None)),
        check_vma=False,
    )
```

profile of v0, /device:TPU:7, one launch (start us, length us, event | category | flops | bytes accessed | tf_op | source)
XLA Modules:
  0.0 358.6 jit_solution(16332044363483749540)
XLA Ops:
  8.2 2.5 collective-permute-start
  13.3 1.9 collective-permute-done.1
  15.5 6.4 %collective-permute-start.3 = (f32[4,34,1,128]{3,0,2,1:T(4,128)S(1)}, f32[4,34,1,128]{3,0,2,1:T(4,128)S(1)}, u32[]{:S(2)}, u32[]{:S(2)}) collective-permute-start(f32[4,34,1,128]{3,0,2,1:T(4,128)S(1)} %copy.535), channel_id=1, source_target_pairs={{1,0},{2,1},{3,2},{4,3},{5,4},{6,5},{7,6},{8,7},{9,8},{10,9},{11,1... | collective-permute-start | bytes 208904 | tf_op jit(solution)/shard_map/ppermute | solution.py:22
  21.9 2.5 collective-permute-done.2
  24.5 1.3 maximum_select_fusion
  28.0 1.2 fusion.43
  29.2 1.5 fusion.44
  33.1 1.5 copy_bitcast_fusion.6
  34.6 1.3 copy_bitcast_fusion.5
  36.2 1.6 fusion.11
  37.9 17.1 %copy.528 = f32[3,32,16,128]{0,3,2,1:T(8,128)} copy(f32[3,32,16,128]{3,2,1,0:T(8,128)} %fusion.11) | data formatting | bytes 1572864
  54.9 43.8 %gather_fusion = bf16[4096,3]{1,0:T(8,128)(2,1)S(1)} fusion(f32[3,32,16,128]{0,3,2,1:T(8,128)} %copy.528, s32[4096]{0:T(1024)S(1)} %reshape.255), kind=kCustom, calls=%fused_computation | custom fusion | bytes 98304 | tf_op jit(solution)/shard_map/gather | solution.py:101
  100.2 1.1 collective-permute-start.4
  102.8 15.8 %all-reduce.2 = (s32[1024]{0:T(1024)S(1)}, s32[1024]{0:T(1024)S(1)}) all-reduce(s32[1024]{0:T(1024)S(1)} %bitcast_dynamic-update-slice_fusion.1, s32[1024]{0:T(1024)S(1)} %bitcast_dynamic-update-slice_fusion), channel_id=3, replica_groups=mesh['gx'=8,'yz'=32] {'yz'}, use_global_device_ids=true, to_apply=%add.1 | all-reduce | flops 2048 | bytes 16384 | tf_op jit(solution)/shard_map/all_gather | solution.py:113
  119.1 1.0 collective-permute-start.6
  120.1 3.9 %collective-permute-start.7 = (f32[34,1,128]{2,0,1:T(8,128)S(1)}, f32[34,1,128]{2,0,1:T(8,128)S(1)}, u32[]{:S(2)}, u32[]{:S(2)}) collective-permute-start(f32[34,1,128]{2,0,1:T(8,128)S(1)} %get-tuple-element.71), channel_id=1, source_target_pairs={{1,0},{2,1},{3,2},{4,3},{5,4},{6,5},{7,6},{8,7},{9,8},{10,9},{11,1... | collective-permute-start | bytes 52232 | tf_op jit(solution)/shard_map/ppermute | solution.py:22
  126.3 45.6 %all-gather.4.cloned.1.call-done = f32[1024,384]{1,0:T(8,128)} async-done(((f32[32,384]{1,0:T(8,128)}), f32[1024,384]{1,0:T(8,128)}) %all-gather.4.cloned.1.call-update) | async-done | bytes 1572880 | tf_op jit(solution)/shard_map/all_gather | solution.py:111
  171.9 2.1 fusion
  174.0 36.3 %all_gather.15 = bf16[1024,384]{1,0:T(8,128)(2,1)S(1)} all-gather(bf16[32,384]{1,0:T(8,128)(2,1)S(1)} %fusion), channel_id=1, replica_groups=mesh['gx'=8,'yz'=32] {'yz'}, dimensions={0}, use_global_device_ids=true | all-gather | bytes 811008 | tf_op jit(solution)/shard_map/all_gather | solution.py:122
  211.3 2.0 copy.532
  213.3 42.0 %scatter_fusion = f32[3,65536]{0,1:T(8,128)} fusion(f32[3,65536]{0,1:T(8,128)} %bitcast.96, s32[4096]{0:T(1024)S(1)} %reshape.269, f32[4096,3]{1,0:T(8,128)} %bitcast.106), kind=kCustom, calls=%fused_computation.2 | custom fusion | flops 12288 | bytes 163840
  255.3 20.3 %slice_reduce_fusion = f32[65536]{0:T(1024)S(1)} fusion(f32[3,65536]{0,1:T(8,128)} %scatter_fusion), kind=kLoop, calls=%fused_computation.3 | loop fusion | bytes 524288 | tf_op jit(solution)/shard_map/slice | solution.py:135
  275.6 18.8 %copy.526 = f32[3,32,16,128]{3,2,1,0:T(8,128)S(1)} copy(f32[3,32,16,128]{0,3,2,1:T(8,128)} %bitcast.97) | data formatting | bytes 1572864 | tf_op jit(solution)/shard_map/scatter-add | solution.py:131
  294.4 17.8 %collective-permute-start.8 = (f32[3,1,16,128]{3,2,1,0:T(8,128)S(1)}, f32[3,1,16,128]{3,2,1,0:T(8,128)S(1)}, u32[]{:S(2)}, u32[]{:S(2)}) collective-permute-start(f32[3,1,16,128]{3,2,1,0:T(8,128)S(1)} %get-tuple-element.48), channel_id=1, source_target_pairs={{0,32},{32,64},{64,96},{96,128},{128,160},{160,192},{192,224},{224... | collective-permute-start | bytes 73736 | tf_op jit(solution)/shard_map/ppermute | solution.py:19
  313.2 3.5 collective-permute-done.9
  316.9 4.8 %collective-permute-start.11 = (f32[3,34,1,128]{3,2,1,0:T(1,128)S(1)}, f32[3,34,1,128]{3,2,1,0:T(1,128)S(1)}, u32[]{:S(2)}, u32[]{:S(2)}) collective-permute-start(f32[3,34,1,128]{3,2,1,0:T(1,128)S(1)} %get-tuple-element.47), channel_id=1, source_target_pairs={{1,0},{2,1},{3,2},{4,3},{5,4},{6,5},{7,6},{8,7},{9,8},{10,9},{11,1... | collective-permute-start | bytes 156680 | tf_op jit(solution)/shard_map/ppermute | solution.py:22
  324.8 1.2 collective-permute-start.12
  326.7 3.5 collective-permute-done.13
  330.3 5.1 %collective-permute-start.15 = (f32[34,1,128]{2,0,1:T(8,128)S(1)}, f32[34,1,128]{2,0,1:T(8,128)S(1)}, u32[]{:S(2)}, u32[]{:S(2)}) collective-permute-start(f32[34,1,128]{2,0,1:T(8,128)S(1)} %get-tuple-element.69), channel_id=1, source_target_pairs={{1,0},{2,1},{3,2},{4,3},{5,4},{6,5},{7,6},{8,7},{9,8},{10,9},{11,1... | collective-permute-start | bytes 52232 | tf_op jit(solution)/shard_map/ppermute | solution.py:22
  335.4 1.1 collective-permute-done.14
  338.9 3.5 collective-permute-done.17
  342.5 5.2 %collective-permute-start.19 = (f32[34,1,128]{2,0,1:T(8,128)S(1)}, f32[34,1,128]{2,0,1:T(8,128)S(1)}, u32[]{:S(2)}, u32[]{:S(2)}) collective-permute-start(f32[34,1,128]{2,0,1:T(8,128)S(1)} %get-tuple-element.67), channel_id=1, source_target_pairs={{1,0},{2,1},{3,2},{4,3},{5,4},{6,5},{7,6},{8,7},{9,8},{10,9},{11,1... | collective-permute-start | bytes 52232 | tf_op jit(solution)/shard_map/ppermute | solution.py:22
  (166 shorter events, 26.2 us)
Async XLA Ops:
  7.2 91.7 %copy-start = (bf16[1,32,128,128]{3,2,1,0:T(8,128)(2,1)S(1)}, bf16[1,32,128,128]{3,2,1,0:T(8,128)(2,1)}, u32[]{:S(2)}) copy-start(bf16[1,32,128,128]{3,2,1,0:T(8,128)(2,1)} %param.9) | copy-start | bytes 3145732
  7.2 8.0 %copy-start.3 = (f32[32,16,128]{2,1,0:T(8,128)S(1)}, f32[32,16,128]{2,1,0:T(8,128)}, u32[]{:S(2)}) copy-start(f32[32,16,128]{2,1,0:T(8,128)} %param.8) | copy-start | bytes 786436
  7.2 8.0 %copy-start.2 = (f32[3,32,16,128]{3,2,1,0:T(8,128)S(1)}, f32[3,32,16,128]{3,2,1,0:T(8,128)}, u32[]{:S(2)}) copy-start(f32[3,32,16,128]{3,2,1,0:T(8,128)} %param.7) | copy-start | bytes 2359300
  7.2 164.7 %all-gather.4.cloned.1.call-start = ((), (), s32[]{:S(2)}) async-start(), calls=%async_computation | async-start | bytes 1622016 | tf_op jit(solution)/shard_map/all_gather | solution.py:111
  8.2 5.1 %collective-permute-start = (f32[4,1,16,128]{3,2,1,0:T(8,128)S(1)}, f32[4,1,16,128]{3,2,1,0:T(8,128)S(1)}, u32[]{:S(2)}, u32[]{:S(2)}) collective-permute-start(f32[4,1,16,128]{3,2,1,0:T(8,128)S(1)} %get-tuple-element.44), channel_id=1, source_target_pairs={{0,32},{32,64},{64,96},{96,128},{128,160},{160,192},{192,224},{224... | collective-permute-start | bytes 98312 | tf_op jit(solution)/shard_map/ppermute | solution.py:19
  10.6 4.6 %collective-permute-start.1 = (f32[4,1,16,128]{3,2,1,0:T(8,128)S(1)}, f32[4,1,16,128]{3,2,1,0:T(8,128)S(1)}, u32[]{:S(2)}, u32[]{:S(2)}) collective-permute-start(f32[4,1,16,128]{3,2,1,0:T(8,128)S(1)} %get-tuple-element.45), channel_id=1, source_target_pairs={{32,0},{64,32},{96,64},{128,96},{160,128},{192,160},{224,192},{0,2... | collective-permute-start | bytes 98312 | tf_op jit(solution)/shard_map/ppermute | solution.py:22
  15.2 9.2 %copy-start.13 = (f32[4,1,16,128]{3,2,1,0:T(8,128)}, f32[4,1,16,128]{3,2,1,0:T(8,128)S(1)}, u32[]{:S(2)}) copy-start(f32[4,1,16,128]{3,2,1,0:T(8,128)S(1)} %collective-permute-done.1) | copy-start | bytes 98308
  15.3 9.0 %collective-permute-start.2 = (f32[4,34,1,128]{3,0,2,1:T(4,128)S(1)}, f32[4,34,1,128]{3,0,2,1:T(4,128)S(1)}, u32[]{:S(2)}, u32[]{:S(2)}) collective-permute-start(f32[4,34,1,128]{3,0,2,1:T(4,128)S(1)} %copy.534), channel_id=1, source_target_pairs={{0,1},{1,2},{2,3},{3,4},{4,5},{5,6},{6,7},{7,8},{8,9},{9,10},{10,1... | collective-permute-start | bytes 208904 | tf_op jit(solution)/shard_map/ppermute | solution.py:19
  15.5 9.0 %collective-permute-start.3 = (f32[4,34,1,128]{3,0,2,1:T(4,128)S(1)}, f32[4,34,1,128]{3,0,2,1:T(4,128)S(1)}, u32[]{:S(2)}, u32[]{:S(2)}) collective-permute-start(f32[4,34,1,128]{3,0,2,1:T(4,128)S(1)} %copy.535), channel_id=1, source_target_pairs={{1,0},{2,1},{3,2},{4,3},{5,4},{6,5},{7,6},{8,7},{9,8},{10,9},{11,1... | collective-permute-start | bytes 208904 | tf_op jit(solution)/shard_map/ppermute | solution.py:22
  98.8 19.9 %copy-start.19 = (s32[32,4]{0,1:T(4,128)S(1)}, s32[32,4]{0,1:T(4,128)}, u32[]{:S(2)}) copy-start(s32[32,4]{0,1:T(4,128)} %get-tuple-element.95) | copy-start | bytes 1540
  98.8 19.9 %copy-start.18 = (s32[32,4]{0,1:T(4,128)S(1)}, s32[32,4]{0,1:T(4,128)}, u32[]{:S(2)}) copy-start(s32[32,4]{0,1:T(4,128)} %get-tuple-element.88) | copy-start | bytes 1540
  98.8 19.9 %copy-start.15 = (s32[32,8]{0,1:T(8,128)S(1)}, s32[32,8]{0,1:T(8,128)}, u32[]{:S(2)}) copy-start(s32[32,8]{0,1:T(8,128)} %get-tuple-element.90) | copy-start | bytes 3076
  98.8 19.9 %copy-start.21 = (s32[3]{0:T(128)S(1)}, s32[3]{0:T(128)}, u32[]{:S(2)}) copy-start(s32[3]{0:T(128)} %constant.64) | copy-start | bytes 40
  98.8 20.0 %copy-start.20 = (s32[3]{0:T(128)S(1)}, s32[3]{0:T(128)}, u32[]{:S(2)}) copy-start(s32[3]{0:T(128)} %constant.67) | copy-start | bytes 40
  98.8 25.2 %copy-start.14 = (f32[1,32,3,128]{3,1,2,0:T(8,128)S(1)}, f32[1,32,3,128]{3,1,2,0:T(8,128)}, u32[]{:S(2)}) copy-start(f32[1,32,3,128]{3,1,2,0:T(8,128)} %param.10) | copy-start | bytes 147460
  99.5 25.7 %copy-start.17 = (pred[18]{0:T(512)(128)(4,1)S(1)}, pred[18]{0:T(512)(128)(4,1)}, u32[]{:S(2)}) copy-start(pred[18]{0:T(512)(128)(4,1)} %copy-done.16) | copy-start | bytes 58
  100.2 18.9 %collective-permute-start.4 = (f32[1,16,128]{2,0,1:T(1,128)S(1)}, f32[1,16,128]{2,0,1:T(1,128)S(1)}, u32[]{:S(2)}, u32[]{:S(2)}) collective-permute-start(f32[1,16,128]{2,0,1:T(1,128)S(1)} %bitcast.120), channel_id=1, source_target_pairs={{0,32},{32,64},{64,96},{96,128},{128,160},{160,192},{192,224},{224... | collective-permute-start | bytes 24584 | tf_op jit(solution)/shard_map/ppermute | solution.py:19
  101.4 17.7 %collective-permute-start.5 = (f32[1,16,128]{2,0,1:T(1,128)S(1)}, f32[1,16,128]{2,0,1:T(1,128)S(1)}, u32[]{:S(2)}, u32[]{:S(2)}) collective-permute-start(f32[1,16,128]{2,0,1:T(1,128)S(1)} %bitcast.119), channel_id=1, source_target_pairs={{32,0},{64,32},{96,64},{128,96},{160,128},{192,160},{224,192},{0,2... | collective-permute-start | bytes 24584 | tf_op jit(solution)/shard_map/ppermute | solution.py:22
  119.1 6.1 %collective-permute-start.6 = (f32[34,1,128]{2,0,1:T(8,128)S(1)}, f32[34,1,128]{2,0,1:T(8,128)S(1)}, u32[]{:S(2)}, u32[]{:S(2)}) collective-permute-start(f32[34,1,128]{2,0,1:T(8,128)S(1)} %get-tuple-element.70), channel_id=1, source_target_pairs={{0,1},{1,2},{2,3},{3,4},{4,5},{5,6},{6,7},{7,8},{8,9},{9,10},{10,1... | collective-permute-start | bytes 52232 | tf_op jit(solution)/shard_map/ppermute | solution.py:19
  120.1 5.1 %collective-permute-start.7 = (f32[34,1,128]{2,0,1:T(8,128)S(1)}, f32[34,1,128]{2,0,1:T(8,128)S(1)}, u32[]{:S(2)}, u32[]{:S(2)}) collective-permute-start(f32[34,1,128]{2,0,1:T(8,128)S(1)} %get-tuple-element.71), channel_id=1, source_target_pairs={{1,0},{2,1},{3,2},{4,3},{5,4},{6,5},{7,6},{8,7},{9,8},{10,9},{11,1... | collective-permute-start | bytes 52232 | tf_op jit(solution)/shard_map/ppermute | solution.py:22
  294.4 18.8 %collective-permute-start.8 = (f32[3,1,16,128]{3,2,1,0:T(8,128)S(1)}, f32[3,1,16,128]{3,2,1,0:T(8,128)S(1)}, u32[]{:S(2)}, u32[]{:S(2)}) collective-permute-start(f32[3,1,16,128]{3,2,1,0:T(8,128)S(1)} %get-tuple-element.48), channel_id=1, source_target_pairs={{0,32},{32,64},{64,96},{96,128},{128,160},{160,192},{192,224},{224... | collective-permute-start | bytes 73736 | tf_op jit(solution)/shard_map/ppermute | solution.py:19
  312.2 4.5 %collective-permute-start.9 = (f32[3,1,16,128]{3,2,1,0:T(8,128)S(1)}, f32[3,1,16,128]{3,2,1,0:T(8,128)S(1)}, u32[]{:S(2)}, u32[]{:S(2)}) collective-permute-start(f32[3,1,16,128]{3,2,1,0:T(8,128)S(1)} %get-tuple-element.49), channel_id=1, source_target_pairs={{32,0},{64,32},{96,64},{128,96},{160,128},{192,160},{224,192},{0,2... | collective-permute-start | bytes 73736 | tf_op jit(solution)/shard_map/ppermute | solution.py:22
  316.8 6.4 %collective-permute-start.10 = (f32[3,34,1,128]{3,2,1,0:T(1,128)S(1)}, f32[3,34,1,128]{3,2,1,0:T(1,128)S(1)}, u32[]{:S(2)}, u32[]{:S(2)}) collective-permute-start(f32[3,34,1,128]{3,2,1,0:T(1,128)S(1)} %get-tuple-element.46), channel_id=1, source_target_pairs={{0,1},{1,2},{2,3},{3,4},{4,5},{5,6},{6,7},{7,8},{8,9},{9,10},{10,1... | collective-permute-start | bytes 156680 | tf_op jit(solution)/shard_map/ppermute | solution.py:19
  316.9 6.3 %collective-permute-start.11 = (f32[3,34,1,128]{3,2,1,0:T(1,128)S(1)}, f32[3,34,1,128]{3,2,1,0:T(1,128)S(1)}, u32[]{:S(2)}, u32[]{:S(2)}) collective-permute-start(f32[3,34,1,128]{3,2,1,0:T(1,128)S(1)} %get-tuple-element.47), channel_id=1, source_target_pairs={{1,0},{2,1},{3,2},{4,3},{5,4},{6,5},{7,6},{8,7},{9,8},{10,9},{11,1... | collective-permute-start | bytes 156680 | tf_op jit(solution)/shard_map/ppermute | solution.py:22
  324.8 2.0 collective-permute-start.12
  325.9 4.3 %collective-permute-start.13 = (f32[1,16,128]{2,0,1:T(1,128)S(1)}, f32[1,16,128]{2,0,1:T(1,128)S(1)}, u32[]{:S(2)}, u32[]{:S(2)}) collective-permute-start(f32[1,16,128]{2,0,1:T(1,128)S(1)} %get-tuple-element.75), channel_id=1, source_target_pairs={{32,0},{64,32},{96,64},{128,96},{160,128},{192,160},{224,192},{0,2... | collective-permute-start | bytes 24584 | tf_op jit(solution)/shard_map/ppermute | solution.py:22
  330.2 6.3 %collective-permute-start.14 = (f32[34,1,128]{2,0,1:T(8,128)S(1)}, f32[34,1,128]{2,0,1:T(8,128)S(1)}, u32[]{:S(2)}, u32[]{:S(2)}) collective-permute-start(f32[34,1,128]{2,0,1:T(8,128)S(1)} %get-tuple-element.68), channel_id=1, source_target_pairs={{0,1},{1,2},{2,3},{3,4},{4,5},{5,6},{6,7},{7,8},{8,9},{9,10},{10,1... | collective-permute-start | bytes 52232 | tf_op jit(solution)/shard_map/ppermute | solution.py:19
  330.3 6.2 %collective-permute-start.15 = (f32[34,1,128]{2,0,1:T(8,128)S(1)}, f32[34,1,128]{2,0,1:T(8,128)S(1)}, u32[]{:S(2)}, u32[]{:S(2)}) collective-permute-start(f32[34,1,128]{2,0,1:T(8,128)S(1)} %get-tuple-element.69), channel_id=1, source_target_pairs={{1,0},{2,1},{3,2},{4,3},{5,4},{6,5},{7,6},{8,7},{9,8},{10,9},{11,1... | collective-permute-start | bytes 52232 | tf_op jit(solution)/shard_map/ppermute | solution.py:22
  337.2 1.7 collective-permute-start.16
  338.1 4.3 %collective-permute-start.17 = (f32[1,16,128]{2,0,1:T(1,128)S(1)}, f32[1,16,128]{2,0,1:T(1,128)S(1)}, u32[]{:S(2)}, u32[]{:S(2)}) collective-permute-start(f32[1,16,128]{2,0,1:T(1,128)S(1)} %get-tuple-element.73), channel_id=1, source_target_pairs={{32,0},{64,32},{96,64},{128,96},{160,128},{192,160},{224,192},{0,2... | collective-permute-start | bytes 24584 | tf_op jit(solution)/shard_map/ppermute | solution.py:22
  342.4 6.4 %collective-permute-start.18 = (f32[34,1,128]{2,0,1:T(8,128)S(1)}, f32[34,1,128]{2,0,1:T(8,128)S(1)}, u32[]{:S(2)}, u32[]{:S(2)}) collective-permute-start(f32[34,1,128]{2,0,1:T(8,128)S(1)} %get-tuple-element.66), channel_id=1, source_target_pairs={{0,1},{1,2},{2,3},{3,4},{4,5},{5,6},{6,7},{7,8},{8,9},{9,10},{10,1... | collective-permute-start | bytes 52232 | tf_op jit(solution)/shard_map/ppermute | solution.py:19
  342.5 6.3 %collective-permute-start.19 = (f32[34,1,128]{2,0,1:T(8,128)S(1)}, f32[34,1,128]{2,0,1:T(8,128)S(1)}, u32[]{:S(2)}, u32[]{:S(2)}) collective-permute-start(f32[34,1,128]{2,0,1:T(8,128)S(1)} %get-tuple-element.67), channel_id=1, source_target_pairs={{1,0},{2,1},{3,2},{4,3},{5,4},{6,5},{7,6},{8,7},{9,8},{10,9},{11,1... | collective-permute-start | bytes 52232 | tf_op jit(solution)/shard_map/ppermute | solution.py:22
  (14 other events, 37.3 us)
Sparse Core Ops, SparseCore 0:
  100.3 71.5 all-gather.3
where the time goes:
time: 360 us; the launch traced here: 359 us
  local copies, waits for them, and re-layouts  120 us (33%)
  waiting for transfers between devices  65.7 us (18%)
  blocking collectives  52.1 us (14%)
  other arithmetic  51.9 us (14%)
  starting transfers between devices  50.3 us (14%)
  between operations  15.5 us (4%)
    all_gather x1, waiting for transfers between devices, body(): lax.all_gather(flat_partial, 'yz', axis=0, tiled=True)  45.6 us
    gather x1, local copies, waits for them, and re-layouts, body(): predicted[:, cell_x, cell_z, cell_y].astype(jnp.bfloat16)  43.8 us
    unnamed x4, other arithmetic  42.2 us
    all_gather x1, blocking collectives, body(): all_force = lax.all_gather(grain_force, 'yz', axis=0, tiled=True)  36.3 us
    ppermute x10, starting transfers between devices, extended(): lax.ppermute(lax.slice_in_dim(block, 0, width, axis=dim), axis, backward)  25.4 us
    ppermute x10, starting transfers between devices, extended(): lax.ppermute(lax.slice_in_dim(block, block.shape[dim] - width, None, axis...  24.9 us
    unnamed x69, local copies, waits for them, and re-layouts  22 us
    slice x1, local copies, waits for them, and re-layouts, body(): forced_velocity[1]  20.3 us
  transfers between devices with their start and end apart: 21, of which 13 were waited for; matrix products, arithmetic and copies ran while one was open for 2% of the time, Pallas kernels for 0%

commit v1 on v0

--- a/solution.py
+++ b/solution.py
@@ -8,6 +8,11 @@
 BY = 8
 step_size = 0.1
 viscosity = 1.5
+
+
+def tiled_gather(array, axis, dim):
+    copies = jnp.concatenate([array] * lax.axis_size(axis), axis=dim)
+    return lax.all_to_all(copies, axis, dim, dim, tiled=True)
 
 
 def extended(block, sides, width):
@@ -110,7 +115,7 @@
     all_partial, all_owner, all_grain = (
         lax.all_gather(flat_partial, "yz", axis=0, tiled=True),
         lax.all_gather(owners, "yz", axis=0, tiled=True),
-        lax.all_gather(grains, "yz", axis=0, tiled=True),
+        tiled_gather(grains, "yz", 0),
     )
     own_tile = lax.axis_index("yz")
     grain_keys = jnp.where(all_owner == own_tile, all_grain, grain_slots)

time: 360 us -> 360 us (level)
  waiting for transfers between devices: 65.7 us -> 54.9 us
  starting transfers between devices: 50.3 us -> 58.6 us
    unnamed x0 -> x1, blocking collectives: none -> 16.3 us
    all_gather x1 -> x0, blocking collectives: 15.8 us -> none  [body(): lax.all_gather(grains, 'yz', axis=0, tiled=True)]
    all_gather x1, waiting for transfers between devices: 45.6 us -> 34.3 us  [body(): lax.all_gather(flat_partial, 'yz', axis=0, tiled=True)]
    all_to_all x0 -> x1, starting transfers between devices: none -> 7.21 us  [tiled_gather(): return lax.all_to_all(copies, axis, dim, dim, tiled=True)]
    unnamed x69 -> x67, local copies, waits for them, and re-layouts: 22 us -> 22 us
  transfers between devices with their start and end apart: 21 -> 22, of which waited for: 13 -> 13; matrix products, arithmetic and copies ran while one was open for 2% -> 2% of each run, Pallas kernels for 0% -> 0%
where the time goes in v1:
time: 360 us; the launch traced here: 359 us
  local copies, waits for them, and re-layouts  122 us (34%)
  starting transfers between devices  58.6 us (16%)
  waiting for transfers between devices  54.9 us (15%)
  other arithmetic  52.6 us (15%)
  blocking collectives  52.6 us (15%)
  between operations  15.5 us (4%)
    gather x1, local copies, waits for them, and re-layouts, body(): predicted[:, cell_x, cell_z, cell_y].astype(jnp.bfloat16)  44 us
    unnamed x4, other arithmetic  42.2 us
    all_gather x1, blocking collectives, body(): all_force = lax.all_gather(grain_force, 'yz', axis=0, tiled=True)  36.3 us
    all_gather x1, waiting for transfers between devices, body(): lax.all_gather(flat_partial, 'yz', axis=0, tiled=True)  34.3 us
    ppermute x10, starting transfers between devices, extended(): lax.ppermute(lax.slice_in_dim(block, block.shape[dim] - width, None, axis...  26 us
    ppermute x10, starting transfers between devices, extended(): lax.ppermute(lax.slice_in_dim(block, 0, width, axis=dim), axis, backward)  25.3 us
    unnamed x67, local copies, waits for them, and re-layouts  22 us
    slice x1, local copies, waits for them, and re-layouts, body(): forced_velocity[1]  20.3 us
  transfers between devices with their start and end apart: 22, of which 13 were waited for; matrix products, arithmetic and copies ran while one was open for 2% of the time, Pallas kernels for 0%

profile of v1, /device:TPU:7, one launch (start us, length us, event | category | flops | bytes accessed | tf_op | source)
XLA Modules:
  0.0 358.8 jit_solution(5711455390793578712)
XLA Ops:
  8.2 2.5 collective-permute-start
  13.3 1.9 collective-permute-done.1
  15.5 6.4 %collective-permute-start.3 = (f32[4,34,1,128]{3,0,2,1:T(4,128)S(1)}, f32[4,34,1,128]{3,0,2,1:T(4,128)S(1)}, u32[]{:S(2)}, u32[]{:S(2)}) collective-permute-start(f32[4,34,1,128]{3,0,2,1:T(4,128)S(1)} %copy.535), channel_id=1, source_target_pairs={{1,0},{2,1},{3,2},{4,3},{5,4},{6,5},{7,6},{8,7},{9,8},{10,9},{11,1... | collective-permute-start | bytes 208904 | tf_op jit(solution)/shard_map/ppermute | solution.py:27
  21.9 2.5 collective-permute-done.2
  24.6 1.3 maximum_select_fusion
  28.0 1.2 fusion.43
  29.2 1.5 fusion.44
  33.2 1.5 copy_bitcast_fusion.6
  34.7 1.3 copy_bitcast_fusion.5
  36.3 1.6 fusion.11
  37.9 17.2 %copy.528 = f32[3,32,16,128]{0,3,2,1:T(8,128)} copy(f32[3,32,16,128]{3,2,1,0:T(8,128)} %fusion.11) | data formatting | bytes 1572864
  55.1 44.0 %gather_fusion = bf16[4096,3]{1,0:T(8,128)(2,1)S(1)} fusion(f32[3,32,16,128]{0,3,2,1:T(8,128)} %copy.528, s32[4096]{0:T(1024)S(1)} %reshape.325), kind=kCustom, calls=%fused_computation | custom fusion | bytes 98304 | tf_op jit(solution)/shard_map/gather | solution.py:106
  101.2 7.2 %all-to-all-start = ((s32[32,32,1]{1,2,0:T(1,128)}), s32[32,32,1]{1,2,0:T(1,128)S(1)}, u32[]{:S(2)}, u32[]{:S(2)}) async-start(s32[32,32,1]{1,2,0:T(1,128)} %concatenate.137), calls=%async_computation | async-start | bytes 32768 | tf_op jit(solution)/shard_map/all_to_all | solution.py:15
  108.5 2.2 collective-permute-start.4
  113.0 16.3 %all-reduce = s32[1024]{0:T(1024)S(1)} all-reduce(s32[1024]{0:T(1024)S(1)} %bitcast_dynamic-update-slice_fusion), channel_id=2, replica_groups=mesh['gx'=8,'yz'=32] {'yz'}, use_global_device_ids=true, to_apply=%add | all-reduce | flops 1024 | bytes 8192
  131.7 3.8 %collective-permute-start.7 = (f32[34,1,128]{2,0,1:T(8,128)S(1)}, f32[34,1,128]{2,0,1:T(8,128)S(1)}, u32[]{:S(2)}, u32[]{:S(2)}) collective-permute-start(f32[34,1,128]{2,0,1:T(8,128)S(1)} %get-tuple-element.69), channel_id=1, source_target_pairs={{1,0},{2,1},{3,2},{4,3},{5,4},{6,5},{7,6},{8,7},{9,8},{10,9},{11,1... | collective-permute-start | bytes 52232 | tf_op jit(solution)/shard_map/ppermute | solution.py:27
  135.5 1.2 collective-permute-done.6
  137.8 34.3 %all-gather.3.cloned.1.call-done = f32[1024,384]{1,0:T(8,128)} async-done(((f32[32,384]{1,0:T(8,128)}), f32[1024,384]{1,0:T(8,128)}) %all-gather.3.cloned.1.call-update) | async-done | bytes 1572880 | tf_op jit(solution)/shard_map/all_gather | solution.py:116
  172.1 2.1 fusion
  174.2 36.3 %all_gather.11 = bf16[1024,384]{1,0:T(8,128)(2,1)S(1)} all-gather(bf16[32,384]{1,0:T(8,128)(2,1)S(1)} %fusion), channel_id=1, replica_groups=mesh['gx'=8,'yz'=32] {'yz'}, dimensions={0}, use_global_device_ids=true | all-gather | bytes 811008 | tf_op jit(solution)/shard_map/all_gather | solution.py:127
  211.5 2.0 copy.532
  213.5 42.0 %scatter_fusion = f32[3,65536]{0,1:T(8,128)} fusion(f32[3,65536]{0,1:T(8,128)} %bitcast.96, s32[4096]{0:T(1024)S(1)} %reshape.339, f32[4096,3]{1,0:T(8,128)} %bitcast.106), kind=kCustom, calls=%fused_computation.2 | custom fusion | flops 12288 | bytes 163840
  255.5 20.3 %slice_reduce_fusion = f32[65536]{0:T(1024)S(1)} fusion(f32[3,65536]{0,1:T(8,128)} %scatter_fusion), kind=kLoop, calls=%fused_computation.3 | loop fusion | bytes 524288 | tf_op jit(solution)/shard_map/slice | solution.py:140
  275.8 18.8 %copy.526 = f32[3,32,16,128]{3,2,1,0:T(8,128)S(1)} copy(f32[3,32,16,128]{0,3,2,1:T(8,128)} %bitcast.97) | data formatting | bytes 1572864 | tf_op jit(solution)/shard_map/scatter-add | solution.py:136
  294.6 17.8 %collective-permute-start.8 = (f32[3,1,16,128]{3,2,1,0:T(8,128)S(1)}, f32[3,1,16,128]{3,2,1,0:T(8,128)S(1)}, u32[]{:S(2)}, u32[]{:S(2)}) collective-permute-start(f32[3,1,16,128]{3,2,1,0:T(8,128)S(1)} %get-tuple-element.46), channel_id=1, source_target_pairs={{0,32},{32,64},{64,96},{96,128},{128,160},{160,192},{192,224},{224... | collective-permute-start | bytes 73736 | tf_op jit(solution)/shard_map/ppermute | solution.py:24
  313.4 3.5 collective-permute-done.9
  317.1 4.8 %collective-permute-start.11 = (f32[3,34,1,128]{3,2,1,0:T(1,128)S(1)}, f32[3,34,1,128]{3,2,1,0:T(1,128)S(1)}, u32[]{:S(2)}, u32[]{:S(2)}) collective-permute-start(f32[3,34,1,128]{3,2,1,0:T(1,128)S(1)} %get-tuple-element.45), channel_id=1, source_target_pairs={{1,0},{2,1},{3,2},{4,3},{5,4},{6,5},{7,6},{8,7},{9,8},{10,9},{11,1... | collective-permute-start | bytes 156680 | tf_op jit(solution)/shard_map/ppermute | solution.py:27
  325.0 1.2 collective-permute-start.12
  326.9 3.5 collective-permute-done.13
  330.5 5.1 %collective-permute-start.15 = (f32[34,1,128]{2,0,1:T(8,128)S(1)}, f32[34,1,128]{2,0,1:T(8,128)S(1)}, u32[]{:S(2)}, u32[]{:S(2)}) collective-permute-start(f32[34,1,128]{2,0,1:T(8,128)S(1)} %get-tuple-element.67), channel_id=1, source_target_pairs={{1,0},{2,1},{3,2},{4,3},{5,4},{6,5},{7,6},{8,7},{9,8},{10,9},{11,1... | collective-permute-start | bytes 52232 | tf_op jit(solution)/shard_map/ppermute | solution.py:27
  339.1 3.5 collective-permute-done.17
  342.7 5.2 %collective-permute-start.19 = (f32[34,1,128]{2,0,1:T(8,128)S(1)}, f32[34,1,128]{2,0,1:T(8,128)S(1)}, u32[]{:S(2)}, u32[]{:S(2)}) collective-permute-start(f32[34,1,128]{2,0,1:T(8,128)S(1)} %get-tuple-element.65), channel_id=1, source_target_pairs={{1,0},{2,1},{3,2},{4,3},{5,4},{6,5},{7,6},{8,7},{9,8},{10,9},{11,1... | collective-permute-start | bytes 52232 | tf_op jit(solution)/shard_map/ppermute | solution.py:27
  (170 shorter events, 29.4 us)
Async XLA Ops:
  7.2 92.1 %copy-start = (bf16[1,32,128,128]{3,2,1,0:T(8,128)(2,1)S(1)}, bf16[1,32,128,128]{3,2,1,0:T(8,128)(2,1)}, u32[]{:S(2)}) copy-start(bf16[1,32,128,128]{3,2,1,0:T(8,128)(2,1)} %param.9) | copy-start | bytes 3145732
  7.2 164.9 %all-gather.3.cloned.1.call-start = ((), (), s32[]{:S(2)}) async-start(), calls=%async_computation.1 | async-start | bytes 1622016 | tf_op jit(solution)/shard_map/all_gather | solution.py:116
  8.2 5.1 %collective-permute-start = (f32[4,1,16,128]{3,2,1,0:T(8,128)S(1)}, f32[4,1,16,128]{3,2,1,0:T(8,128)S(1)}, u32[]{:S(2)}, u32[]{:S(2)}) collective-permute-start(f32[4,1,16,128]{3,2,1,0:T(8,128)S(1)} %get-tuple-element.42), channel_id=1, source_target_pairs={{0,32},{32,64},{64,96},{96,128},{128,160},{160,192},{192,224},{224... | collective-permute-start | bytes 98312 | tf_op jit(solution)/shard_map/ppermute | solution.py:24
  10.6 4.6 %collective-permute-start.1 = (f32[4,1,16,128]{3,2,1,0:T(8,128)S(1)}, f32[4,1,16,128]{3,2,1,0:T(8,128)S(1)}, u32[]{:S(2)}, u32[]{:S(2)}) collective-permute-start(f32[4,1,16,128]{3,2,1,0:T(8,128)S(1)} %get-tuple-element.43), channel_id=1, source_target_pairs={{32,0},{64,32},{96,64},{128,96},{160,128},{192,160},{224,192},{0,2... | collective-permute-start | bytes 98312 | tf_op jit(solution)/shard_map/ppermute | solution.py:27
  15.3 9.0 %collective-permute-start.2 = (f32[4,34,1,128]{3,0,2,1:T(4,128)S(1)}, f32[4,34,1,128]{3,0,2,1:T(4,128)S(1)}, u32[]{:S(2)}, u32[]{:S(2)}) collective-permute-start(f32[4,34,1,128]{3,0,2,1:T(4,128)S(1)} %copy.534), channel_id=1, source_target_pairs={{0,1},{1,2},{2,3},{3,4},{4,5},{5,6},{6,7},{7,8},{8,9},{9,10},{10,1... | collective-permute-start | bytes 208904 | tf_op jit(solution)/shard_map/ppermute | solution.py:24
  15.5 9.0 %collective-permute-start.3 = (f32[4,34,1,128]{3,0,2,1:T(4,128)S(1)}, f32[4,34,1,128]{3,0,2,1:T(4,128)S(1)}, u32[]{:S(2)}, u32[]{:S(2)}) collective-permute-start(f32[4,34,1,128]{3,0,2,1:T(4,128)S(1)} %copy.535), channel_id=1, source_target_pairs={{1,0},{2,1},{3,2},{4,3},{5,4},{6,5},{7,6},{8,7},{9,8},{10,9},{11,1... | collective-permute-start | bytes 208904 | tf_op jit(solution)/shard_map/ppermute | solution.py:27
  99.2 11.5 %copy-start.24 = (u32[256]{0:T(256)S(1)}, u32[256]{0:T(256)}, u32[]{:S(2)}) copy-start(u32[256]{0:T(256)} %constant.93) | copy-start | bytes 3076
  99.2 12.8 %copy-start.19 = (s32[32,4]{0,1:T(4,128)S(1)}, s32[32,4]{0,1:T(4,128)}, u32[]{:S(2)}) copy-start(s32[32,4]{0,1:T(4,128)} %get-tuple-element.93) | copy-start | bytes 1540
  99.2 12.8 %copy-start.18 = (s32[32,4]{0,1:T(4,128)S(1)}, s32[32,4]{0,1:T(4,128)}, u32[]{:S(2)}) copy-start(s32[32,4]{0,1:T(4,128)} %get-tuple-element.86) | copy-start | bytes 1540
  99.2 12.8 %copy-start.15 = (s32[32,8]{0,1:T(8,128)S(1)}, s32[32,8]{0,1:T(8,128)}, u32[]{:S(2)}) copy-start(s32[32,8]{0,1:T(8,128)} %get-tuple-element.88) | copy-start | bytes 3076
  99.2 12.8 %copy-start.21 = (s32[3]{0:T(128)S(1)}, s32[3]{0:T(128)}, u32[]{:S(2)}) copy-start(s32[3]{0:T(128)} %constant.64) | copy-start | bytes 40
  99.2 12.9 %copy-start.20 = (s32[3]{0:T(128)S(1)}, s32[3]{0:T(128)}, u32[]{:S(2)}) copy-start(s32[3]{0:T(128)} %constant.67) | copy-start | bytes 40
  99.2 13.0 %copy-start.23 = (s32[1,32,1]{1,2,0:T(1,128)S(1)}, s32[1,32,1]{1,2,0:T(1,128)}, u32[]{:S(2)}) copy-start(s32[1,32,1]{1,2,0:T(1,128)} %param.11) | copy-start | bytes 388
  99.2 13.3 %copy-start.14 = (f32[1,32,3,128]{3,1,2,0:T(8,128)S(1)}, f32[1,32,3,128]{3,1,2,0:T(8,128)}, u32[]{:S(2)}) copy-start(f32[1,32,3,128]{3,1,2,0:T(8,128)} %param.10) | copy-start | bytes 147460
  99.9 36.8 %copy-start.17 = (pred[18]{0:T(512)(128)(4,1)S(1)}, pred[18]{0:T(512)(128)(4,1)}, u32[]{:S(2)}) copy-start(pred[18]{0:T(512)(128)(4,1)} %copy-done.16) | copy-start | bytes 58
  101.2 28.1 %all-to-all-start = ((s32[32,32,1]{1,2,0:T(1,128)}), s32[32,32,1]{1,2,0:T(1,128)S(1)}, u32[]{:S(2)}, u32[]{:S(2)}) async-start(s32[32,32,1]{1,2,0:T(1,128)} %concatenate.137), calls=%async_computation | async-start | bytes 32768 | tf_op jit(solution)/shard_map/all_to_all | solution.py:15
  108.5 22.1 %collective-permute-start.4 = (f32[1,16,128]{2,0,1:T(1,128)S(1)}, f32[1,16,128]{2,0,1:T(1,128)S(1)}, u32[]{:S(2)}, u32[]{:S(2)}) collective-permute-start(f32[1,16,128]{2,0,1:T(1,128)S(1)} %bitcast.120), channel_id=1, source_target_pairs={{0,32},{32,64},{64,96},{96,128},{128,160},{160,192},{192,224},{224... | collective-permute-start | bytes 24584 | tf_op jit(solution)/shard_map/ppermute | solution.py:24
  110.7 19.9 %collective-permute-start.5 = (f32[1,16,128]{2,0,1:T(1,128)S(1)}, f32[1,16,128]{2,0,1:T(1,128)S(1)}, u32[]{:S(2)}, u32[]{:S(2)}) collective-permute-start(f32[1,16,128]{2,0,1:T(1,128)S(1)} %bitcast.119), channel_id=1, source_target_pairs={{32,0},{64,32},{96,64},{128,96},{160,128},{192,160},{224,192},{0,2... | collective-permute-start | bytes 24584 | tf_op jit(solution)/shard_map/ppermute | solution.py:27
  130.6 6.1 %collective-permute-start.6 = (f32[34,1,128]{2,0,1:T(8,128)S(1)}, f32[34,1,128]{2,0,1:T(8,128)S(1)}, u32[]{:S(2)}, u32[]{:S(2)}) collective-permute-start(f32[34,1,128]{2,0,1:T(8,128)S(1)} %get-tuple-element.68), channel_id=1, source_target_pairs={{0,1},{1,2},{2,3},{3,4},{4,5},{5,6},{6,7},{7,8},{8,9},{9,10},{10,1... | collective-permute-start | bytes 52232 | tf_op jit(solution)/shard_map/ppermute | solution.py:24
  131.7 5.0 %collective-permute-start.7 = (f32[34,1,128]{2,0,1:T(8,128)S(1)}, f32[34,1,128]{2,0,1:T(8,128)S(1)}, u32[]{:S(2)}, u32[]{:S(2)}) collective-permute-start(f32[34,1,128]{2,0,1:T(8,128)S(1)} %get-tuple-element.69), channel_id=1, source_target_pairs={{1,0},{2,1},{3,2},{4,3},{5,4},{6,5},{7,6},{8,7},{9,8},{10,9},{11,1... | collective-permute-start | bytes 52232 | tf_op jit(solution)/shard_map/ppermute | solution.py:27
  294.6 18.8 %collective-permute-start.8 = (f32[3,1,16,128]{3,2,1,0:T(8,128)S(1)}, f32[3,1,16,128]{3,2,1,0:T(8,128)S(1)}, u32[]{:S(2)}, u32[]{:S(2)}) collective-permute-start(f32[3,1,16,128]{3,2,1,0:T(8,128)S(1)} %get-tuple-element.46), channel_id=1, source_target_pairs={{0,32},{32,64},{64,96},{96,128},{128,160},{160,192},{192,224},{224... | collective-permute-start | bytes 73736 | tf_op jit(solution)/shard_map/ppermute | solution.py:24
  312.4 4.5 %collective-permute-start.9 = (f32[3,1,16,128]{3,2,1,0:T(8,128)S(1)}, f32[3,1,16,128]{3,2,1,0:T(8,128)S(1)}, u32[]{:S(2)}, u32[]{:S(2)}) collective-permute-start(f32[3,1,16,128]{3,2,1,0:T(8,128)S(1)} %get-tuple-element.47), channel_id=1, source_target_pairs={{32,0},{64,32},{96,64},{128,96},{160,128},{192,160},{224,192},{0,2... | collective-permute-start | bytes 73736 | tf_op jit(solution)/shard_map/ppermute | solution.py:27
  317.0 6.4 %collective-permute-start.10 = (f32[3,34,1,128]{3,2,1,0:T(1,128)S(1)}, f32[3,34,1,128]{3,2,1,0:T(1,128)S(1)}, u32[]{:S(2)}, u32[]{:S(2)}) collective-permute-start(f32[3,34,1,128]{3,2,1,0:T(1,128)S(1)} %get-tuple-element.44), channel_id=1, source_target_pairs={{0,1},{1,2},{2,3},{3,4},{4,5},{5,6},{6,7},{7,8},{8,9},{9,10},{10,1... | collective-permute-start | bytes 156680 | tf_op jit(solution)/shard_map/ppermute | solution.py:24
  317.1 6.3 %collective-permute-start.11 = (f32[3,34,1,128]{3,2,1,0:T(1,128)S(1)}, f32[3,34,1,128]{3,2,1,0:T(1,128)S(1)}, u32[]{:S(2)}, u32[]{:S(2)}) collective-permute-start(f32[3,34,1,128]{3,2,1,0:T(1,128)S(1)} %get-tuple-element.45), channel_id=1, source_target_pairs={{1,0},{2,1},{3,2},{4,3},{5,4},{6,5},{7,6},{8,7},{9,8},{10,9},{11,1... | collective-permute-start | bytes 156680 | tf_op jit(solution)/shard_map/ppermute | solution.py:27
  325.0 2.0 collective-permute-start.12
  326.1 4.3 %collective-permute-start.13 = (f32[1,16,128]{2,0,1:T(1,128)S(1)}, f32[1,16,128]{2,0,1:T(1,128)S(1)}, u32[]{:S(2)}, u32[]{:S(2)}) collective-permute-start(f32[1,16,128]{2,0,1:T(1,128)S(1)} %get-tuple-element.73), channel_id=1, source_target_pairs={{32,0},{64,32},{96,64},{128,96},{160,128},{192,160},{224,192},{0,2... | collective-permute-start | bytes 24584 | tf_op jit(solution)/shard_map/ppermute | solution.py:27
  330.4 6.3 %collective-permute-start.14 = (f32[34,1,128]{2,0,1:T(8,128)S(1)}, f32[34,1,128]{2,0,1:T(8,128)S(1)}, u32[]{:S(2)}, u32[]{:S(2)}) collective-permute-start(f32[34,1,128]{2,0,1:T(8,128)S(1)} %get-tuple-element.66), channel_id=1, source_target_pairs={{0,1},{1,2},{2,3},{3,4},{4,5},{5,6},{6,7},{7,8},{8,9},{9,10},{10,1... | collective-permute-start | bytes 52232 | tf_op jit(solution)/shard_map/ppermute | solution.py:24
  330.5 6.2 %collective-permute-start.15 = (f32[34,1,128]{2,0,1:T(8,128)S(1)}, f32[34,1,128]{2,0,1:T(8,128)S(1)}, u32[]{:S(2)}, u32[]{:S(2)}) collective-permute-start(f32[34,1,128]{2,0,1:T(8,128)S(1)} %get-tuple-element.67), channel_id=1, source_target_pairs={{1,0},{2,1},{3,2},{4,3},{5,4},{6,5},{7,6},{8,7},{9,8},{10,9},{11,1... | collective-permute-start | bytes 52232 | tf_op jit(solution)/shard_map/ppermute | solution.py:27
  337.4 1.7 collective-permute-start.16
  338.3 4.3 %collective-permute-start.17 = (f32[1,16,128]{2,0,1:T(1,128)S(1)}, f32[1,16,128]{2,0,1:T(1,128)S(1)}, u32[]{:S(2)}, u32[]{:S(2)}) collective-permute-start(f32[1,16,128]{2,0,1:T(1,128)S(1)} %get-tuple-element.71), channel_id=1, source_target_pairs={{32,0},{64,32},{96,64},{128,96},{160,128},{192,160},{224,192},{0,2... | collective-permute-start | bytes 24584 | tf_op jit(solution)/shard_map/ppermute | solution.py:27
  342.6 6.4 %collective-permute-start.18 = (f32[34,1,128]{2,0,1:T(8,128)S(1)}, f32[34,1,128]{2,0,1:T(8,128)S(1)}, u32[]{:S(2)}, u32[]{:S(2)}) collective-permute-start(f32[34,1,128]{2,0,1:T(8,128)S(1)} %get-tuple-element.64), channel_id=1, source_target_pairs={{0,1},{1,2},{2,3},{3,4},{4,5},{5,6},{6,7},{7,8},{8,9},{9,10},{10,1... | collective-permute-start | bytes 52232 | tf_op jit(solution)/shard_map/ppermute | solution.py:24
  342.7 6.3 %collective-permute-start.19 = (f32[34,1,128]{2,0,1:T(8,128)S(1)}, f32[34,1,128]{2,0,1:T(8,128)S(1)}, u32[]{:S(2)}, u32[]{:S(2)}) collective-permute-start(f32[34,1,128]{2,0,1:T(8,128)S(1)} %get-tuple-element.65), channel_id=1, source_target_pairs={{1,0},{2,1},{3,2},{4,3},{5,4},{6,5},{7,6},{8,7},{9,8},{10,9},{11,1... | collective-permute-start | bytes 52232 | tf_op jit(solution)/shard_map/ppermute | solution.py:27
  (15 other events, 61.4 us)
Sparse Core Ops, SparseCore 0:
  100.7 71.3 all-gather.2
